TPU v7x, 32 devices: a whole 2x2x4 slice. The times are simulated.
32 devices in a mesh: req: 8 (over y, x, core), tp: 4 (over z).
Axes of the slice: x: 2, y: 2, z: 4, core: 2. Of those that a mesh axis runs over, the one named last changes fastest.
Arguments:
- queries: bfloat16 [1536, 2560], P('req', 'tp'), may hold values from -5 to 5
- new_keys: bfloat16 [1536, 512], P('req', 'tp'), may hold values from -5 to 5
- new_values: bfloat16 [1536, 512], P('req', 'tp'), may hold values from -5 to 5
- key_pages: bfloat16 [512, 64, 512], P('req', None, 'tp'), may hold values from -5 to 5
- value_pages: bfloat16 [512, 64, 512], P('req', None, 'tp'), may hold values from -5 to 5
- page_table: int32 [32, 16], P('req'), may hold values from 0 to 511, as said below
- cache_lengths: int32 [32], P('req'), may hold values from 2 to 1024, as said below
- parents: int32 [32, 48], P('req'), may hold values from -1 to 46, as said below
- residual: bfloat16 [1536, 2560], P('req'), may hold values from -6 to 6
- out_weight: bfloat16 [2560, 2560], P('tp'), may hold values from -0.125 to 0.125
- norm_gain: float32 [2560], replicated, may hold values from 0.1 to 1.9
- router_weight: float32 [2560, 16], replicated, may hold values from -0.125 to 0.125
- routes: int32 [1536, 6], P('req'), may hold values from 0 to 15, all different within a row; in each aligned block of 192 rows (0 to 191, 192 to 383, ...) at most 91 rows name the same one
- expert_gate_up: bfloat16 [16, 2560, 2, 1536], P('req', None, None, 'tp'), may hold values from -0.125 to 0.125
- expert_down: bfloat16 [16, 1536, 2560], P('req', 'tp'), may hold values from -0.15625 to 0.15625
- shared_gate_up: bfloat16 [2560, 2, 1536], P(None, None, 'tp'), may hold values from -0.125 to 0.125
- shared_down: bfloat16 [1536, 2560], P('tp'), may hold values from -0.15625 to 0.15625
Outputs:
- layer_out: bfloat16 [1536, 2560], P('req', 'tp')
Inputs may be any that keep to these rules, and one draw needn't show every extreme that they name: `page_table`: the pages of the 4 requests of the d-th block of 4 rows are the d-th block of 64 pages of the pool, each named once. `cache_lengths`: some request holds 1024 positions. parents[r, 0] = -1, and 0 <= parents[r, i] < i for i >= 1. `routes`: A token's 6 experts differ. In each aligned block of 192 rows no expert is named by more than 91 rows, and in some block one expert is named by exactly 91.
All inputs are finite; a program needn't handle non-finite values.
Results may differ from a plain program's by a relative error of at most 0.02.
Values may be sent and summed in bfloat16 or wider, within the bound.
No kernel may reach another device: no remote copies, remote signals or barrier semaphores. Data moves between devices by JAX's collectives and lax.ppermute only.
A program may use at most 128 MiB of HBM per device.

v0:
```python
import math
import jax
import jax.numpy as jnp
from jax import lax
from jax.sharding import PartitionSpec as P

QH = 20
KVH = 4
HD = 128
EPSILON = 1e-06
NEGATIVE = -1e30


def rounded(values):
    return lax.optimization_barrier(values.astype(jnp.bfloat16)).astype(jnp.float32)


def ancestors(parents):
    tree_size = parents.shape[-1]
    position = jnp.arange(tree_size, dtype=jnp.int32)
    adjacency = (parents[..., :, None] == position[None, :]) | (
        position[:, None] == position[None, :]
    )
    closure = adjacency.astype(jnp.float32)
    for doubling in range(max(1, (tree_size - 1).bit_length())):
        closure = jnp.minimum(
            jnp.einsum("...ij,...jk->...ik", closure, closure, precision=lax.Precision.HIGHEST), 1.0
        )
    return closure > 0.5


def tree_attention(queries, cache_keys, cache_values, new_keys, new_values, lengths, allowed):
    scaling = 1.0 / math.sqrt(queries.shape[-1])
    cache_scores = (
        jnp.einsum("rtkgd,rckd->rkgtc", queries, cache_keys, preferred_element_type=jnp.float32)
        * scaling
    )
    tree_scores = (
        jnp.einsum("rtkgd,rskd->rkgts", queries, new_keys, preferred_element_type=jnp.float32)
        * scaling
    )
    live = jnp.arange(cache_keys.shape[1], dtype=jnp.int32)[None, :] < lengths[:, None]
    cache_scores = jnp.where(live[:, None, None, None, :], cache_scores, NEGATIVE)
    tree_scores = jnp.where(allowed[:, None, None, :, :], tree_scores, NEGATIVE)
    highest = jnp.maximum(jnp.max(cache_scores, axis=-1), jnp.max(tree_scores, axis=-1))[..., None]
    cache_exp = jnp.exp(cache_scores - highest)
    tree_exp = jnp.exp(tree_scores - highest)
    denominator = (jnp.sum(cache_exp, axis=-1) + jnp.sum(tree_exp, axis=-1))[..., None]
    cache_probs = (cache_exp / denominator).astype(jnp.bfloat16)
    tree_probs = (tree_exp / denominator).astype(jnp.bfloat16)
    mixed = jnp.einsum(
        "rkgtc,rckd->rtkgd", cache_probs, cache_values, preferred_element_type=jnp.float32
    )
    mixed = mixed + jnp.einsum(
        "rkgts,rskd->rtkgd", tree_probs, new_values, preferred_element_type=jnp.float32
    )
    return mixed.astype(jnp.bfloat16).reshape(queries.shape[0], queries.shape[1], -1)


def place_rows(routes, experts_local, groups, capacity):
    flat_expert = routes.reshape(-1)
    expert_ids = jnp.arange(experts_local * groups, dtype=jnp.int32)
    onehot = (flat_expert[:, None] == expert_ids[None, :]).astype(jnp.int32)
    earlier = jnp.cumsum(onehot, axis=0) - onehot
    rank = jnp.sum(earlier * onehot, axis=1)
    owner = flat_expert // experts_local
    local_expert = flat_expert % experts_local
    return (local_expert * groups + owner) * capacity + rank


def fill_outbox(row_values, slot_index, top_count, lead_shape):
    repeated = jnp.repeat(row_values, top_count, axis=0)
    outbox = jnp.zeros(
        (lead_shape[0] * lead_shape[1] * lead_shape[2], row_values.shape[1]), row_values.dtype
    )
    outbox = outbox.at[slot_index].set(repeated)
    return outbox.reshape(lead_shape + (row_values.shape[1],))


def shards(
    queries,
    new_keys,
    new_values,
    key_pages,
    value_pages,
    page_table,
    cache_lengths,
    parents,
    residual,
    out_weight,
    norm_gain,
    router_weight,
    routes,
    expert_gate_up,
    expert_down,
    shared_gate_up,
    shared_down,
):
    groups = lax.axis_size("req")
    tp_count = lax.axis_size("tp")
    requests = parents.shape[0]
    tree_size = parents.shape[1]
    row_count = requests * tree_size
    kv_local = new_keys.shape[1] // HD
    head_ratio = QH // KVH
    model_width = residual.shape[1]
    part_width = model_width // tp_count
    pages_dev = key_pages.shape[0]
    local_pages = page_table - lax.axis_index("req") * pages_dev
    cache_keys = key_pages[local_pages].reshape(requests, -1, kv_local, HD)
    cache_values = value_pages[local_pages].reshape(requests, -1, kv_local, HD)
    head_outputs = tree_attention(
        queries.reshape(requests, tree_size, kv_local, head_ratio, HD),
        cache_keys,
        cache_values,
        new_keys.reshape(requests, tree_size, kv_local, HD),
        new_values.reshape(requests, tree_size, kv_local, HD),
        cache_lengths,
        ancestors(parents),
    )
    attn_terms = jnp.dot(
        head_outputs.reshape(row_count, -1), out_weight, preferred_element_type=jnp.float32
    )
    column = lax.axis_index("tp") * part_width
    experts_local = expert_gate_up.shape[0]
    top_count = routes.shape[1]
    expert_count = experts_local * groups
    capacity = max(10 * requests, row_count * top_count * 5 // (4 * expert_count) + 1)
    slot_index = place_rows(routes, experts_local, groups, capacity)
    lead_shape = (experts_local, groups, capacity)
    attn_out = lax.psum(attn_terms.astype(jnp.bfloat16), "tp").astype(jnp.float32)
    hidden = rounded(residual.astype(jnp.float32) + attn_out)
    rstd = lax.rsqrt(jnp.mean(hidden * hidden, axis=1, keepdims=True) + EPSILON)
    normed = hidden * rstd * norm_gain
    logits = jnp.dot(normed, router_weight, precision=lax.Precision.HIGHEST)
    normed_bf = normed.astype(jnp.bfloat16)
    hidden_part = lax.dynamic_slice_in_dim(hidden, column, part_width, 1)
    outbox = fill_outbox(normed_bf, slot_index, top_count, lead_shape)
    arrived = lax.all_to_all(outbox, "req", split_axis=1, concat_axis=1, tiled=True)
    arrived = arrived.reshape(experts_local, groups * capacity, model_width)
    gate_up = jnp.einsum(
        "emd,edcf->emcf", arrived, expert_gate_up, preferred_element_type=jnp.float32
    )
    act = (jax.nn.silu(gate_up[:, :, 0]) * gate_up[:, :, 1]).astype(jnp.bfloat16)
    partial_value = rounded(
        jnp.einsum("emf,efd->emd", act, expert_down, preferred_element_type=jnp.float32)
    )
    summed = lax.psum_scatter(
        partial_value.astype(jnp.bfloat16), "tp", scatter_dimension=2, tiled=True
    )
    outputs = summed.reshape(experts_local, groups, capacity, part_width)
    returned = lax.all_to_all(outputs, "req", split_axis=1, concat_axis=1, tiled=True).reshape(
        -1, part_width
    )
    picked = returned[slot_index].astype(jnp.float32).reshape(row_count, top_count, part_width)
    expert_ids = jnp.arange(expert_count, dtype=jnp.int32)
    chosen = jnp.sum(
        jnp.where(routes[:, :, None] == expert_ids[None, None, :], logits[:, None, :], 0.0), axis=-1
    )
    gate_values = jax.nn.sigmoid(chosen)
    gate_values = gate_values / jnp.sum(gate_values, axis=1, keepdims=True)
    routed = jnp.sum(picked * gate_values[:, :, None], axis=1)
    shared_gu = jnp.einsum(
        "td,dcf->tcf", normed_bf, shared_gate_up, preferred_element_type=jnp.float32
    )
    shared_act = (jax.nn.silu(shared_gu[:, 0]) * shared_gu[:, 1]).astype(jnp.bfloat16)
    shared_terms = jnp.dot(shared_act, shared_down, preferred_element_type=jnp.float32)
    shared_out = lax.psum_scatter(
        shared_terms.astype(jnp.bfloat16), "tp", scatter_dimension=1, tiled=True
    ).astype(jnp.float32)
    return (hidden_part + shared_out + routed).astype(jnp.bfloat16)


def solution(mesh):
    in_specs = (
        P("req", "tp"),
        P("req", "tp"),
        P("req", "tp"),
        P("req", None, "tp"),
        P("req", None, "tp"),
        P("req", None),
        P("req"),
        P("req", None),
        P("req", None),
        P("tp", None),
        P(),
        P(),
        P("req", None),
        P("req", None, None, "tp"),
        P("req", "tp", None),
        P(None, None, "tp"),
        P("tp", None),
    )
    out_specs = P("req", "tp")
    return jax.shard_map(shards, mesh=mesh, in_specs=in_specs, out_specs=out_specs, check_vma=False)
```

profile of v0, /device:TPU:0, one launch (start us, length us, event | category | flops | bytes accessed | tf_op | source)
XLA Modules:
  0.0 486.2 jit_solution(5703992235077245131)
XLA Ops:
  8.3 2.0 reshape.306
  12.5 2.9 gather_fusion.1
  15.4 2.1 bitcast_reduce_fusion
  20.5 2.9 gather_fusion
  23.4 3.5 fusion.11
  27.4 1.9 convolution_convert_fusion.2
  30.1 4.5 reduce-window.6
  35.5 46.5 %all-reduce.2.cloned.1.call-done = bf16[192,2560]{1,0:T(8,128)(2,1)} async-done(((bf16[192,2560]{1,0:T(8,128)(2,1)}), bf16[192,2560]{1,0:T(8,128)(2,1)}) %all-reduce.2.cloned.1.call-update) | async-done | bytes 983056 | tf_op jit(solution)/shard_map/psum | solution.py:131
  82.0 1.7 add_convert_fusion
  84.3 4.0 broadcast_in_dim.72
  88.3 10.2 %reshape.347 = bf16[1152,2560]{1,0:T(8,128)(2,1)} reshape(bf16[192,6,2560]{2,1,0:T(8,128)(2,1)} %broadcast_in_dim.72) | data formatting | bytes 11796480 | tf_op jit(solution)/shard_map/reshape | solution.py:72
  98.5 17.2 %scatter_custom_fusion = bf16[1456,2560]{1,0:T(8,128)(2,1)} fusion(s32[1152]{0:T(1024)S(1)} %fusion.48, bf16[1152,2560]{1,0:T(8,128)(2,1)} %reshape.347, bf16[]{:T(256)} %constant.73.clone.1), kind=kCustom, calls=%fused_computation.18 | custom fusion | bytes 7455232 | tf_op jit(solution)/shard_map/scatter | solution.py:76
  115.7 6.3 %reshape.314 = bf16[2,8,91,2560]{3,2,1,0:T(8,128)(2,1)} reshape(bf16[1456,2560]{1,0:T(8,128)(2,1)} %scatter_custom_fusion) | data formatting | bytes 14909440 | tf_op jit(solution)/shard_map/reshape | solution.py:77
  121.9 27.5 %copy.66 = bf16[2,8,91,2560]{3,0,2,1:T(2,128)(2,1)S(1)} copy(bf16[2,8,91,2560]{3,2,1,0:T(8,128)(2,1)} %reshape.314) | data formatting | bytes 14909440 | tf_op jit(solution)/shard_map/reshape | solution.py:77
  149.4 87.5 %all_to_all.10 = bf16[2,8,91,2560]{3,0,2,1:T(2,128)(2,1)S(1)} all-to-all(bf16[2,8,91,2560]{3,0,2,1:T(2,128)(2,1)S(1)} %copy.66), channel_id=1, replica_groups=mesh['req'=8,'tp'=4] {'req'}, dimensions={1} | all-to-all | bytes 14909440 | tf_op jit(solution)/shard_map/all_to_all | solution.py:139
  236.9 9.0 %fusion = f32[2,728,2,384]{3,1,2,0:T(8,128)S(1)} fusion(bf16[2,2560,2,384]{3,2,1,0:T(2,128)(2,1)} %param.30, bf16[2,728,2560,1]{2,0,1,3:T(2,128)(2,1)S(1)} %bitcast.150), kind=kOutput, calls=%fused_computation.4 | convolution fusion | flops 5725224960 | bytes 19791872 | tf_op jit(solution)/shard_map/emd,edcf->emcf/dot_general | solution.py:141
  245.9 6.1 %convolution_convert_fusion = bf16[2,728,2560]{2,1,0:T(8,128)(2,1)} fusion(bf16[2,384,2560]{2,1,0:T(8,128)(2,1)S(1)} %copy-done.9, f32[2,728,2,384]{3,1,2,0:T(8,128)S(1)} %fusion), kind=kOutput, calls=%fused_computation.7 | convolution fusion | flops 2869694464 | bytes 15859712 | tf_op jit(solution)/shard_map/emf,efd->emd/dot_general | solution.py:146
  252.0 20.1 %copy.85 = bf16[2,728,2560]{1,0,2:T(2,128)(2,1)} copy(bf16[2,728,2560]{2,1,0:T(8,128)(2,1)} %convolution_convert_fusion) | data formatting | bytes 14909440
  272.1 18.3 %reshape.365 = bf16[2560,1456]{1,0:T(8,128)(2,1)} reshape(bf16[2560,2,728]{2,1,0:T(2,128)(2,1)} %bitcast.148) | data formatting | bytes 14909440
  290.8 3.2 fusion.4
  296.1 128.2 %reduce-scatter.9.cloned.1.call-done = bf16[640,1456]{1,0:T(8,128)(2,1)} async-done(((bf16[2560,1456]{1,0:T(8,128)(2,1)}), bf16[640,1456]{1,0:T(8,128)(2,1)}) %reduce-scatter.9.cloned.1.call-update) | async-done | bytes 1863696
  424.4 5.2 %reshape.366 = bf16[640,2,728]{2,1,0:T(2,128)(2,1)S(1)} reshape(bf16[640,1456]{1,0:T(8,128)(2,1)} %reduce-scatter.9.cloned.1.call-done) | data formatting | bytes 3727360
  429.5 5.0 %copy.82 = bf16[2,728,640]{2,0,1:T(2,128)(2,1)} copy(bf16[2,728,640]{1,0,2:T(2,128)(2,1)S(1)} %bitcast.149) | data formatting | bytes 3727360 | tf_op jit(solution)/shard_map/reshape | solution.py:151
  434.5 3.8 all-to-all-start.1
  439.8 1.8 fusion.14
  442.4 16.1 %reduce-scatter.7.cloned.1.call-done = bf16[640,192]{1,0:T(8,128)(2,1)} async-done(((bf16[2560,192]{1,0:T(8,128)(2,1)}), bf16[640,192]{1,0:T(8,128)(2,1)}) %reduce-scatter.7.cloned.1.call-update) | async-done | bytes 245776
  459.7 2.7 all-to-all-done.1
  463.9 1.8 reshape.317
  465.8 4.8 gather_fusion.2
  470.6 4.0 reshape.318
  474.5 3.4 multiply_reduce_fusion
  477.9 1.8 add_convert_fusion.1
  (74 shorter events, 17.0 us)
Async XLA Ops:
  6.5 20.8 %copy-start = (bf16[640,2560]{1,0:T(8,128)(2,1)S(1)}, bf16[640,2560]{1,0:T(8,128)(2,1)}, u32[]{:S(2)}) copy-start(bf16[640,2560]{1,0:T(8,128)(2,1)} %param.26) | copy-start | bytes 9830404
  6.5 75.4 %all-reduce.2.cloned.1.call-start = ((), (), s32[]{:S(2)}) async-start(), calls=%async_computation.4 | async-start | bytes 1966080 | tf_op jit(solution)/shard_map/psum | solution.py:131
  11.9 5.6 %copy-start.6 = (bf16[192,128]{1,0:T(8,128)(2,1)S(1)}, bf16[192,128]{1,0:T(8,128)(2,1)}, u32[]{:S(2)}) copy-start(bf16[192,128]{1,0:T(8,128)(2,1)} %param.18) | copy-start | bytes 147460
  15.4 2.2 copy-start.3
  17.6 1.9 copy-start.2
  18.0 2.4 copy-start.4
  23.4 3.5 copy-start.5
  23.4 3.5 copy-start.12
  26.9 2.6 copy-start.7
  29.3 54.7 %copy-start.8 = (f32[2560]{0:T(1024)S(1)}, f32[2560]{0:T(1024)}, u32[]{:S(2)}) copy-start(f32[2560]{0:T(1024)} %param.27) | copy-start | bytes 30724
  29.3 395.0 %reduce-scatter.9.cloned.1.call-start = ((), (), s32[]{:S(2)}) async-start(), calls=%async_computation.6 | async-start | bytes 9830400
  236.9 9.0 %copy-start.9 = (bf16[2,384,2560]{2,1,0:T(8,128)(2,1)S(1)}, bf16[2,384,2560]{2,1,0:T(8,128)(2,1)}, u32[]{:S(2)}) copy-start(bf16[2,384,2560]{2,1,0:T(8,128)(2,1)} %param.31) | copy-start | bytes 11796484
  290.5 168.1 %reduce-scatter.7.cloned.1.call-start = ((), (), s32[]{:S(2)}) async-start(), calls=%async_computation.5 | async-start | bytes 1638400
  290.8 3.2 copy-start.10
  434.5 5.3 %copy-start.11 = (f32[2560,16]{0,1:T(8,128)S(1)}, f32[2560,16]{0,1:T(8,128)}, u32[]{:S(2)}) copy-start(f32[2560,16]{0,1:T(8,128)} %param.28) | copy-start | bytes 491524
  434.5 27.9 %all-to-all-start.1 = ((bf16[2,8,91,640]{3,0,2,1:T(2,128)(2,1)}), bf16[2,8,91,640]{3,0,2,1:T(2,128)(2,1)S(1)}, u32[]{:S(2)}, u32[]{:S(2)}) async-start(bf16[2,8,91,640]{3,0,2,1:T(2,128)(2,1)} %bitcast.151), calls=%async_computation.1 | async-start | bytes 3727360 | tf_op jit(solution)/shard_map/all_to_all | solution.py:152
  470.6 9.1 %copy-start.1 = (bf16[640,2560]{1,0:T(8,128)(2,1)S(1)}, bf16[640,2560]{1,0:T(8,128)(2,1)}, u32[]{:S(2)}) copy-start(bf16[640,2560]{1,0:T(8,128)(2,1)} %param.26) | copy-start | bytes 9830404
Sparse Core Ops, SparseCore 0:
  29.4 52.4 all-reduce.1
  290.6 133.7 reduce-scatter.8
  426.8 31.7 reduce-scatter.6
where the time goes:
time: 488 us; the launch traced here: 486 us
  waiting for transfers between devices  194 us (40%)
  local copies, waits for them, and re-layouts  140 us (29%)
  blocking collectives  87.5 us (18%)
  matrix products  31.1 us (6%)
  other arithmetic  16.7 us (3%)
  between operations  13.5 us (3%)
    unnamed x5, waiting for transfers between devices  144 us
    all_to_all x1, blocking collectives, shards(): lax.all_to_all(outbox, 'req', split_axis=1, concat_axis=1, tiled=True)  87.5 us
    unnamed x32, local copies, waits for them, and re-layouts  47.7 us
    psum x1, waiting for transfers between devices, shards(): lax.psum(attn_terms.astype(jnp.bfloat16), 'tp').astype(jnp.float32)  46.5 us
    reshape x2, local copies, waits for them, and re-layouts, fill_outbox(): return outbox.reshape(lead_shape + (row_values.shape[1],))  33.8 us
    scatter x1, local copies, waits for them, and re-layouts, fill_outbox(): outbox = outbox.at[slot_index].set(repeated)  17.2 us
    reshape x1, local copies, waits for them, and re-layouts, fill_outbox(): repeated = jnp.repeat(row_values, top_count, axis=0)  10.2 us
  transfers between devices with their start and end apart: 4, of which 4 were waited for; matrix products, arithmetic and copies ran while one was open for 5% of the time, Pallas kernels for 0%

commit v1 on v0

--- a/solution.py
+++ b/solution.py
@@ -136,7 +136,10 @@
     normed_bf = normed.astype(jnp.bfloat16)
     hidden_part = lax.dynamic_slice_in_dim(hidden, column, part_width, 1)
     outbox = fill_outbox(normed_bf, slot_index, top_count, lead_shape)
-    arrived = lax.all_to_all(outbox, "req", split_axis=1, concat_axis=1, tiled=True)
+    arrived = jnp.concatenate(
+        lax.all_to_all(jnp.stack(jnp.split(outbox, lax.axis_size("req"), axis=1)), "req", 0, 0),
+        axis=1,
+    )
     arrived = arrived.reshape(experts_local, groups * capacity, model_width)
     gate_up = jnp.einsum(
         "emd,edcf->emcf", arrived, expert_gate_up, preferred_element_type=jnp.float32

time: 488 us -> 507 us (1.039)
  local copies, waits for them, and re-layouts: 140 us -> 155 us
    another operation x1 -> x3, local copies, waits for them, and re-layouts: 1.97 us -> 36.1 us  [the longest x2 34.2 us: shards(): jnp.stack(jnp.split(outbox, lax.axis_size('req'), axis=1))]
    reshape x2 -> x1, local copies, waits for them, and re-layouts: 33.8 us -> 6.25 us  [fill_outbox(): return outbox.reshape(lead_shape + (row_values.shape[1],))]
    unnamed x32 -> x41, local copies, waits for them, and re-layouts: 47.7 us -> 56.7 us
where the time goes in v1:
time: 507 us; the launch traced here: 505 us
  waiting for transfers between devices  194 us (38%)
  local copies, waits for them, and re-layouts  155 us (31%)
  blocking collectives  87.5 us (17%)
  matrix products  34.4 us (7%)
  other arithmetic  16.7 us (3%)
  between operations  13.5 us (3%)
    unnamed x5, waiting for transfers between devices  144 us
    all_to_all x1, blocking collectives, shards(): lax.all_to_all(jnp.stack(jnp.split(outbox, lax.axis_size('req'), axis=1))...  87.5 us
    unnamed x41, local copies, waits for them, and re-layouts  56.7 us
    psum x1, waiting for transfers between devices, shards(): lax.psum(attn_terms.astype(jnp.bfloat16), 'tp').astype(jnp.float32)  46.5 us
    another operation x2, local copies, waits for them, and re-layouts, shards(): jnp.stack(jnp.split(outbox, lax.axis_size('req'), axis=1))  34.2 us
    scatter x1, local copies, waits for them, and re-layouts, fill_outbox(): outbox = outbox.at[slot_index].set(repeated)  17.2 us
    dot_general x1, matrix products, shards(): jnp.einsum('emf,efd->emd', act, expert_down, preferred_element_type=jnp.f...  10.5 us
    reshape x1, local copies, waits for them, and re-layouts, fill_outbox(): repeated = jnp.repeat(row_values, top_count, axis=0)  10.2 us
  transfers between devices with their start and end apart: 4, of which 4 were waited for; matrix products, arithmetic and copies ran while one was open for 5% of the time, Pallas kernels for 0%

profile of v1, /device:TPU:0, one launch (start us, length us, event | category | flops | bytes accessed | tf_op | source)
XLA Modules:
  0.0 505.1 jit_solution(12956136291536164954)
XLA Ops:
  8.3 2.0 reshape.306
  12.5 2.9 gather_fusion.1
  15.4 2.1 bitcast_reduce_fusion
  20.5 2.9 gather_fusion
  23.4 3.5 fusion.11
  27.4 1.9 convolution_convert_fusion.2
  30.1 4.5 reduce-window.6
  35.5 46.5 %all-reduce.2.cloned.1.call-done = bf16[192,2560]{1,0:T(8,128)(2,1)} async-done(((bf16[192,2560]{1,0:T(8,128)(2,1)}), bf16[192,2560]{1,0:T(8,128)(2,1)}) %all-reduce.2.cloned.1.call-update) | async-done | bytes 983056 | tf_op jit(solution)/shard_map/psum | solution.py:131
  82.0 1.7 add_convert_fusion
  84.3 4.0 broadcast_in_dim.72
  88.3 10.2 %reshape.347 = bf16[1152,2560]{1,0:T(8,128)(2,1)} reshape(bf16[192,6,2560]{2,1,0:T(8,128)(2,1)} %broadcast_in_dim.72) | data formatting | bytes 11796480 | tf_op jit(solution)/shard_map/reshape | solution.py:72
  98.5 17.2 %scatter_custom_fusion = bf16[1456,2560]{1,0:T(8,128)(2,1)} fusion(s32[1152]{0:T(1024)S(1)} %fusion.56, bf16[1152,2560]{1,0:T(8,128)(2,1)} %reshape.347, bf16[]{:T(256)} %constant.73.clone.1), kind=kCustom, calls=%fused_computation.18 | custom fusion | bytes 7455232 | tf_op jit(solution)/shard_map/scatter | solution.py:76
  115.7 6.3 %reshape.314 = bf16[2,8,91,2560]{3,2,1,0:T(8,128)(2,1)} reshape(bf16[1456,2560]{1,0:T(8,128)(2,1)} %scatter_custom_fusion) | data formatting | bytes 14909440 | tf_op jit(solution)/shard_map/reshape | solution.py:77
  132.3 32.7 %copy.95 = bf16[8,2,1,91,2560]{4,1,3,2,0:T(2,128)(2,1)S(1)} copy(bf16[8,2,1,91,2560]{4,3,1,2,0:T(8,128)(2,1)S(1)} %fusion.25) | data formatting | bytes 14909440 | tf_op jit(solution)/shard_map/stack | solution.py:140
  165.0 87.5 %all_to_all.10 = bf16[8,2,1,91,2560]{4,1,3,2,0:T(2,128)(2,1)S(1)} all-to-all(bf16[8,2,1,91,2560]{4,1,3,2,0:T(2,128)(2,1)S(1)} %copy.95), channel_id=1, replica_groups=mesh['req'=8,'tp'=4] {'req'}, dimensions={0} | all-to-all | bytes 14909440 | tf_op jit(solution)/shard_map/all_to_all | solution.py:140
  252.5 7.9 %fusion = f32[2,728,2,384]{3,1,2,0:T(8,128)} fusion(bf16[2,2560,2,384]{3,2,1,0:T(2,128)(2,1)S(1)} %bitcast.209, bf16[2,728,2560,1]{2,0,1,3:T(2,128)(2,1)S(1)} %bitcast.198), kind=kOutput, calls=%fused_computation.4 | convolution fusion | flops 5725224960 | bytes 19791872 | tf_op jit(solution)/shard_map/emd,edcf->emcf/dot_general | solution.py:144
  260.4 10.5 %convolution_convert_fusion = bf16[2,728,2560]{2,1,0:T(8,128)(2,1)} fusion(bf16[2,384,2560]{2,1,0:T(8,128)(2,1)} %param.31, f32[2,728,2,384]{3,1,2,0:T(8,128)} %fusion), kind=kOutput, calls=%fused_computation.7 | convolution fusion | flops 2869694464 | bytes 15859712 | tf_op jit(solution)/shard_map/emf,efd->emd/dot_general | solution.py:149
  270.9 20.1 %copy.114 = bf16[2,728,2560]{1,0,2:T(2,128)(2,1)} copy(bf16[2,728,2560]{2,1,0:T(8,128)(2,1)} %convolution_convert_fusion) | data formatting | bytes 14909440
  290.9 18.3 %reshape.365 = bf16[2560,1456]{1,0:T(8,128)(2,1)} reshape(bf16[2560,2,728]{2,1,0:T(2,128)(2,1)} %bitcast.196) | data formatting | bytes 14909440
  309.6 3.2 fusion.4
  315.0 128.2 %reduce-scatter.9.cloned.1.call-done = bf16[640,1456]{1,0:T(8,128)(2,1)} async-done(((bf16[2560,1456]{1,0:T(8,128)(2,1)}), bf16[640,1456]{1,0:T(8,128)(2,1)}) %reduce-scatter.9.cloned.1.call-update) | async-done | bytes 1863696
  443.2 5.2 %reshape.366 = bf16[640,2,728]{2,1,0:T(2,128)(2,1)S(1)} reshape(bf16[640,1456]{1,0:T(8,128)(2,1)} %reduce-scatter.9.cloned.1.call-done) | data formatting | bytes 3727360
  448.4 5.0 copy.111
  453.3 3.8 all-to-all-start.1
  458.6 1.8 fusion.14
  461.3 16.1 %reduce-scatter.7.cloned.1.call-done = bf16[640,192]{1,0:T(8,128)(2,1)} async-done(((bf16[2560,192]{1,0:T(8,128)(2,1)}), bf16[640,192]{1,0:T(8,128)(2,1)}) %reduce-scatter.7.cloned.1.call-update) | async-done | bytes 245776
  478.5 2.7 all-to-all-done.1
  482.8 1.8 reshape.317
  484.6 4.8 gather_fusion.2
  489.4 4.0 reshape.318
  493.4 3.4 multiply_reduce_fusion
  496.7 1.8 add_convert_fusion.1
  (85 shorter events, 27.3 us)
Async XLA Ops:
  6.5 20.8 %copy-start = (bf16[640,2560]{1,0:T(8,128)(2,1)S(1)}, bf16[640,2560]{1,0:T(8,128)(2,1)}, u32[]{:S(2)}) copy-start(bf16[640,2560]{1,0:T(8,128)(2,1)} %param.26) | copy-start | bytes 9830404
  6.5 75.4 %all-reduce.2.cloned.1.call-start = ((), (), s32[]{:S(2)}) async-start(), calls=%async_computation.4 | async-start | bytes 1966080 | tf_op jit(solution)/shard_map/psum | solution.py:131
  11.9 5.6 %copy-start.6 = (bf16[192,128]{1,0:T(8,128)(2,1)S(1)}, bf16[192,128]{1,0:T(8,128)(2,1)}, u32[]{:S(2)}) copy-start(bf16[192,128]{1,0:T(8,128)(2,1)} %param.18) | copy-start | bytes 147460
  15.4 2.2 copy-start.3
  17.6 1.9 copy-start.2
  18.0 2.4 copy-start.4
  23.4 3.5 copy-start.5
  23.4 3.5 copy-start.11
  26.9 2.6 copy-start.7
  29.3 54.7 %copy-start.8 = (f32[2560]{0:T(1024)S(1)}, f32[2560]{0:T(1024)}, u32[]{:S(2)}) copy-start(f32[2560]{0:T(1024)} %param.27) | copy-start | bytes 30724
  29.3 413.9 %reduce-scatter.9.cloned.1.call-start = ((), (), s32[]{:S(2)}) async-start(), calls=%async_computation.6 | async-start | bytes 9830400
  130.8 121.7 %slice-start = ((s8[7864320]{0:T(1024)(128)(4,1)}), s8[4194304]{0:T(1024)(128)(4,1)S(1)}, s32[]{:S(2)}) async-start(s8[7864320]{0:T(1024)(128)(4,1)} %bitcast.208), calls=%async_computation.7 | async-start | bytes 8388608
  132.3 120.2 %slice-start.1 = ((s8[7864320]{0:T(1024)(128)(4,1)}), s8[3670016]{0:T(1024)(128)(4,1)S(1)}, s32[]{:S(2)}) async-start(s8[7864320]{0:T(1024)(128)(4,1)} %bitcast.208), calls=%async_computation.8 | async-start | bytes 7340032
  309.3 168.1 %reduce-scatter.7.cloned.1.call-start = ((), (), s32[]{:S(2)}) async-start(), calls=%async_computation.5 | async-start | bytes 1638400
  309.6 3.2 copy-start.9
  453.3 5.3 %copy-start.10 = (f32[2560,16]{0,1:T(8,128)S(1)}, f32[2560,16]{0,1:T(8,128)}, u32[]{:S(2)}) copy-start(f32[2560,16]{0,1:T(8,128)} %param.28) | copy-start | bytes 491524
  453.3 27.9 %all-to-all-start.1 = ((bf16[2,8,91,640]{3,0,2,1:T(2,128)(2,1)}), bf16[2,8,91,640]{3,0,2,1:T(2,128)(2,1)S(1)}, u32[]{:S(2)}, u32[]{:S(2)}) async-start(bf16[2,8,91,640]{3,0,2,1:T(2,128)(2,1)} %bitcast.199), calls=%async_computation.1 | async-start | bytes 3727360 | tf_op jit(solution)/shard_map/all_to_all | solution.py:155
  489.4 9.1 %copy-start.1 = (bf16[640,2560]{1,0:T(8,128)(2,1)S(1)}, bf16[640,2560]{1,0:T(8,128)(2,1)}, u32[]{:S(2)}) copy-start(bf16[640,2560]{1,0:T(8,128)(2,1)} %param.26) | copy-start | bytes 9830404
Sparse Core Ops, SparseCore 0:
  29.4 52.4 all-reduce.1
  309.4 133.7 reduce-scatter.8
  445.6 31.7 reduce-scatter.6
